TPU v7x, 256 devices: a whole 4x4x8 slice. The times are simulated.
256 devices in a mesh: con: 4 (over z_hi), grid: 64 (over z_lo, y, x, core).
Axes of the slice: x: 4, y: 4, z: 8 (z_hi: 4, z_lo: 2; z = z_hi * 2 + z_lo), core: 2. Of those that a mesh axis runs over, the one named last changes fastest.
Arguments:
- velocity: bfloat16 [8, 2, 4096, 4096], P('con', None, 'grid'), may hold values from -6 to 6
- seed_adjoint: bfloat16 [8, 2, 4096, 4096], P('con', None, 'grid'), may hold values from -6 to 6
- land_mask: int32 [4096, 4096], P('grid'), may hold values from 0 to 2
- inv_x: bfloat16 [32, 128, 128], replicated, may hold values from -0.5 to 0.5
- inv_y: bfloat16 [32, 128, 128], replicated, may hold values from -0.5 to 0.5
- weights: float32 [8], P('con'), may hold values from 0.05 to 0.5
Outputs:
- velocity_adjoint: float32 [8, 2, 4096, 4096], P('con', None, 'grid')
Inputs may be any that keep to these rules, and one draw needn't show every extreme that they name: `land_mask`: 0 marks land, 1 a wet interior cell, 2 an open-boundary cell whose value is prescribed.
All inputs are finite; a program needn't handle non-finite values.
Results may differ from a plain program's by a relative error of at most 0.0039.
Values may be sent and summed in bfloat16 or wider, within the bound.
No kernel may reach another device: no remote copies, remote signals or barrier semaphores. Data moves between devices by JAX's collectives and lax.ppermute only.
A program may use at most 64 MiB of HBM per device.

v0:
```python
import jax
import jax.numpy as jnp
from jax import lax
from jax.sharding import PartitionSpec as P

BLK = 128


def local(velocity, seed_adjoint, land_mask, inv_x, inv_y, weights):
    nblocks = inv_x.shape[0]
    con_local = velocity.shape[0]
    cols_local = seed_adjoint.shape[2]
    full_side = seed_adjoint.shape[3]
    rows_local = velocity.shape[2]
    vel_float = velocity.astype(jnp.float32)
    weight_full = weights[:, None, None, None]
    local_squares = jnp.sum(weight_full * vel_float * vel_float, axis=(0, 1))
    squares = lax.psum(local_squares, "con")
    sea_bool = land_mask == 1
    sea_float = sea_bool.astype(jnp.float32)
    sea_turned = jnp.swapaxes(sea_bool, 0, 1).astype(jnp.bfloat16)
    blocks_x = seed_adjoint.reshape(con_local, 2, cols_local, nblocks, BLK)
    across = jnp.einsum("cpyki,kji->cpykj", blocks_x, inv_x, preferred_element_type=jnp.float32)
    across = across.astype(jnp.bfloat16).reshape(con_local, 2, cols_local, full_side)
    arrived = lax.all_to_all(across, "grid", split_axis=3, concat_axis=2, tiled=True)
    count = arrived.shape[0]
    masked = arrived * sea_turned[None, None]
    blocks_y = masked.reshape(count, 2, nblocks, BLK, rows_local)
    solved = jnp.einsum("cpkiu,kji->cpukj", blocks_y, inv_y, preferred_element_type=jnp.float32)
    rhs_adjoint = solved.reshape(count, 2, rows_local, nblocks * BLK)
    local_inner = jnp.sum(rhs_adjoint * vel_float, axis=(0, 1))
    inner = lax.psum(local_inner.astype(jnp.bfloat16), "con").astype(jnp.float32)
    speed = jnp.sqrt(0.25 + squares)
    first = -0.5 * sea_float * speed * rhs_adjoint
    second = -0.5 * sea_float * weight_full * vel_float * inner / speed
    return first + second


def solution(mesh):
    return jax.shard_map(
        local,
        mesh=mesh,
        in_specs=(
            P("con", None, "grid", None),
            P("con", None, "grid", None),
            P("grid", None),
            P(),
            P(),
            P("con"),
        ),
        out_specs=P("con", None, "grid", None),
        check_vma=False,
    )
```

profile of v0, /device:TPU:1, one launch (start us, length us, event | category | flops | bytes accessed | tf_op | source)
XLA Modules:
  0.0 237.2 jit_solution(3635252358337494409)
XLA Ops:
  6.5 1.6 copy-done
  8.1 3.3 %convert_bitcast_fusion = bf16[2,2,64,32,128]{4,2,1,0,3:T(8,128)(2,1)} fusion(bf16[32,128,128]{2,1,0:T(8,128)(2,1)} %param.9, bf16[2,2,64,4096]{3,2,1,0:T(8,128)(2,1)S(1)} %copy-done), kind=kOutput, calls=%fused_computation.16 | convolution fusion | flops 269484032 | bytes 5242880 | tf_op jit(solution)/shard_map/cpyki,kji->cpykj/dot_general | solution.py:23
  11.4 10.0 %copy.22 = bf16[2,2,64,32,128]{2,1,0,4,3:T(2,128)(2,1)} copy(bf16[2,2,64,32,128]{4,2,1,0,3:T(8,128)(2,1)} %convert_bitcast_fusion) | data formatting | bytes 4194304 | tf_op jit(solution)/shard_map/reshape | solution.py:24
  21.4 9.8 %reshape.31 = bf16[64,2,8192]{2,1,0:T(2,128)(2,1)} reshape(bf16[4096,2,2,64]{3,2,1,0:T(2,128)(2,1)} %bitcast.46) | data formatting | bytes 4194304
  31.3 10.5 %all-to-all-start = ((bf16[64,2,8192]{2,1,0:T(2,128)(2,1)}), bf16[64,2,8192]{2,1,0:T(2,128)(2,1)}, u32[]{:S(2)}, u32[]{:S(2)}) async-start(bf16[64,2,8192]{2,1,0:T(2,128)(2,1)} %reshape.31), calls=%async_computation | async-start | bytes 4194304 | tf_op jit(solution)/shard_map/all_to_all | solution.py:25
  41.8 0.2 all-reduce.5.cloned.1.call-start
  42.0 1.4 broadcast_select_fusion
  43.6 0.9 copy.26
  44.5 24.8 %all-to-all-done = bf16[64,2,8192]{2,1,0:T(2,128)(2,1)} async-done(((bf16[64,2,8192]{2,1,0:T(2,128)(2,1)}), bf16[64,2,8192]{2,1,0:T(2,128)(2,1)}, u32[]{:S(2)}, u32[]{:S(2)}) %all-to-all-start) | async-done | bytes 2097184 | tf_op jit(solution)/shard_map/all_to_all | solution.py:25
  69.2 9.8 %reshape.32 = bf16[4096,2,2,64]{3,2,1,0:T(2,128)(2,1)} reshape(bf16[64,2,8192]{2,1,0:T(2,128)(2,1)} %all-to-all-done) | data formatting | bytes 4194304
  79.0 6.8 %copy.38 = bf16[2,2,64,64,64]{2,3,4,1,0:T(8,128)(2,1)} copy(bf16[2,2,64,64,64]{2,1,0,4,3:T(2,128)(2,1)} %bitcast.47) | data formatting | bytes 4194304 | tf_op jit(solution)/shard_map/all_to_all | solution.py:25
  85.8 6.2 %all_to_all.16 = bf16[2,2,32,128,64]{3,2,4,1,0:T(8,128)(2,1)} reshape(bf16[2,2,64,64,64]{3,2,4,1,0:T(8,128)(2,1)} %bitcast.48) | data formatting | bytes 4194304 | tf_op jit(solution)/shard_map/all_to_all | solution.py:25
  92.0 2.0 broadcast_multiply_fusion.1
  94.0 1.2 convolution_bitcast_fusion
  95.2 0.4 copy-done.3
  95.6 2.4 %fusion.4 = (bf16[64,4096]{1,0:T(8,128)(2,1)}, f32[64,4096]{1,0:T(8,128)}) fusion(bf16[2,2,64,4096]{3,2,1,0:T(8,128)(2,1)S(1)} %copy-done.3, f32[32,2,2,8,8,128]{5,4,3,2,1,0:T(8,128)S(1)} %convolution_bitcast_fusion, f32[2]{0:T(128)S(1)} %copy-done.5), kind=kLoop, calls=%fused_computation.8 | loop fusion | flops 5767168 | bytes 7864328 | tf_op jit(solution)/shard_map/reduce_sum | solution.py:31
  98.1 0.7 all-reduce.3.cloned.1.call-update
  98.8 1.6 broadcast_multiply_fusion
  100.5 52.3 %all-reduce.5.cloned.1.call-done = bf16[64,4096]{1,0:T(8,128)(2,1)} async-done(((bf16[64,4096]{1,0:T(8,128)(2,1)}), bf16[64,4096]{1,0:T(8,128)(2,1)}) %all-reduce.5.cloned.1.call-update) | async-done | bytes 524304 | tf_op jit(solution)/shard_map/psum | solution.py:32
  152.8 1.1 convert_element_type.25
  153.9 68.7 %all-reduce.3.cloned.1.call-done = f32[64,4096]{1,0:T(8,128)} async-done(((f32[64,4096]{1,0:T(8,128)}), f32[64,4096]{1,0:T(8,128)}) %all-reduce.3.cloned.1.call-update) | async-done | bytes 1048592 | tf_op jit(solution)/shard_map/psum | solution.py:18
  222.6 1.8 fusion.13
  224.4 0.1 copy-done.2
  224.5 5.9 %fusion.3 = f32[2,2,64,4096]{3,2,1,0:T(8,128)} fusion(bf16[2,2,64,4096]{3,2,1,0:T(8,128)(2,1)} %param.6, f32[32,2,2,8,8,128]{5,4,3,2,1,0:T(8,128)} %copy-done.1, f32[64,4096]{1,0:T(8,128)S(1)} %get-tuple-element.10, f32[64,4096]{1,0:T(8,128)S(1)} %convert_element_type.25, f32[2,64,4096]{2,1,0:T(8,128)S(1)} %copy-done.2, f32[64,4096]{1,0:T(8,128)S(1)} %get-tuple-element.9), kind=kLoop, calls=%fused_computation.7 | loop fusion | flops 6291456 | bytes 15728640 | tf_op jit(solution)/shard_map/add | solution.py:36
  (12 shorter events, 0.2 us)
Async XLA Ops:
  6.5 1.6 copy-start
  31.3 38.0 %all-to-all-start = ((bf16[64,2,8192]{2,1,0:T(2,128)(2,1)}), bf16[64,2,8192]{2,1,0:T(2,128)(2,1)}, u32[]{:S(2)}, u32[]{:S(2)}) async-start(bf16[64,2,8192]{2,1,0:T(2,128)(2,1)} %reshape.31), calls=%async_computation | async-start | bytes 4194304 | tf_op jit(solution)/shard_map/all_to_all | solution.py:25
  41.8 111.0 %all-reduce.5.cloned.1.call-start = ((), (), s32[]{:S(2)}) async-start(), calls=%async_computation.2 | async-start | bytes 1048576 | tf_op jit(solution)/shard_map/psum | solution.py:32
  92.0 2.0 copy-start.4
  94.0 1.6 copy-start.3
  94.0 1.6 copy-start.5
  95.6 2.4 %copy-start.1 = (f32[32,2,2,8,8,128]{5,4,3,2,1,0:T(8,128)}, f32[32,2,2,8,8,128]{5,4,3,2,1,0:T(8,128)S(1)}, u32[]{:S(2)}) copy-start(f32[32,2,2,8,8,128]{5,4,3,2,1,0:T(8,128)S(1)} %convolution_bitcast_fusion) | copy-start | bytes 12582916
  98.1 124.5 %all-reduce.3.cloned.1.call-start = ((), (), s32[]{:S(2)}) async-start(), calls=%async_computation.1 | async-start | bytes 2097152 | tf_op jit(solution)/shard_map/psum | solution.py:18
  222.6 1.9 copy-start.2
Sparse Core Ops, SparseCore 0:
  98.2 54.5 all-reduce.4
  155.4 67.1 all-reduce.2
where the time goes:
time: 238 us; the launch traced here: 237 us
  waiting for transfers between devices  146 us (61%)
  local copies, waits for them, and re-layouts  45.7 us (19%)
  other arithmetic  16.3 us (7%)
  between operations  13.5 us (6%)
  starting transfers between devices  10.8 us (5%)
  matrix products  4.45 us (2%)
    psum x1, waiting for transfers between devices, local(): squares = lax.psum(local_squares, 'con')  68.7 us
    psum x1, waiting for transfers between devices, local(): lax.psum(local_inner.astype(jnp.bfloat16), 'con').astype(jnp.float32)  52.3 us
    all_to_all x1, waiting for transfers between devices, local(): lax.all_to_all(across, 'grid', split_axis=3, concat_axis=2, tiled=True)  24.8 us
    unnamed x15, local copies, waits for them, and re-layouts  22.7 us
    all_to_all x2, local copies, waits for them, and re-layouts, local(): lax.all_to_all(across, 'grid', split_axis=3, concat_axis=2, tiled=True)  13 us
    all_to_all x1, starting transfers between devices, local(): lax.all_to_all(across, 'grid', split_axis=3, concat_axis=2, tiled=True)  10.5 us
    reshape x1, local copies, waits for them, and re-layouts, local(): across.astype(jnp.bfloat16).reshape(con_local, 2, cols_local, full_side)  10 us
    add x1, other arithmetic, local(): return first + second  5.88 us
  transfers between devices with their start and end apart: 3, of which 3 were waited for; matrix products, arithmetic and copies ran while one was open for 2% of the time, Pallas kernels for 0%

commit v1 on v0

--- a/solution.py
+++ b/solution.py
@@ -15,7 +15,7 @@
     vel_float = velocity.astype(jnp.float32)
     weight_full = weights[:, None, None, None]
     local_squares = jnp.sum(weight_full * vel_float * vel_float, axis=(0, 1))
-    squares = lax.psum(local_squares, "con")
+    squares = jnp.sum(lax.all_gather(local_squares, "con"), axis=0)
     sea_bool = land_mask == 1
     sea_float = sea_bool.astype(jnp.float32)
     sea_turned = jnp.swapaxes(sea_bool, 0, 1).astype(jnp.bfloat16)

time: 238 us -> 259 us (1.088)
  the two profiles are of different devices: /device:TPU:1 before, /device:TPU:36 now
where the time goes in v1:
time: 259 us; the launch traced here: 258 us
  waiting for transfers between devices  165 us (64%)
  local copies, waits for them, and re-layouts  47 us (18%)
  other arithmetic  18.6 us (7%)
  between operations  13.5 us (5%)
  starting transfers between devices  9.46 us (4%)
  matrix products  4.47 us (2%)
    all_gather x1, waiting for transfers between devices, local(): squares = jnp.sum(lax.all_gather(local_squares, 'con'), axis=0)  85.9 us
    psum x1, waiting for transfers between devices, local(): lax.psum(local_inner.astype(jnp.bfloat16), 'con').astype(jnp.float32)  53.3 us
    all_to_all x1, waiting for transfers between devices, local(): lax.all_to_all(across, 'grid', split_axis=3, concat_axis=2, tiled=True)  24.6 us
    unnamed x17, local copies, waits for them, and re-layouts  24 us
    all_to_all x2, local copies, waits for them, and re-layouts, local(): lax.all_to_all(across, 'grid', split_axis=3, concat_axis=2, tiled=True)  13 us
    reshape x1, local copies, waits for them, and re-layouts, local(): across.astype(jnp.bfloat16).reshape(con_local, 2, cols_local, full_side)  10 us
    all_to_all x1, starting transfers between devices, local(): lax.all_to_all(across, 'grid', split_axis=3, concat_axis=2, tiled=True)  9.2 us
    add x1, other arithmetic, local(): return first + second  5.92 us
  transfers between devices with their start and end apart: 3, of which 3 were waited for; matrix products, arithmetic and copies ran while one was open for 2% of the time, Pallas kernels for 0%

profile of v1, /device:TPU:36, one launch (start us, length us, event | category | flops | bytes accessed | tf_op | source)
XLA Modules:
  0.0 257.6 jit_solution(4225432053347429878)
XLA Ops:
  6.5 1.6 copy-done
  8.1 3.3 %convert_bitcast_fusion = bf16[2,2,64,32,128]{4,2,1,0,3:T(8,128)(2,1)} fusion(bf16[32,128,128]{2,1,0:T(8,128)(2,1)} %param.9, bf16[2,2,64,4096]{3,2,1,0:T(8,128)(2,1)S(1)} %copy-done), kind=kOutput, calls=%fused_computation.16 | convolution fusion | flops 269484032 | bytes 5242880 | tf_op jit(solution)/shard_map/cpyki,kji->cpykj/dot_general | solution.py:23
  11.4 10.0 %copy.28 = bf16[2,2,64,32,128]{2,1,0,4,3:T(2,128)(2,1)} copy(bf16[2,2,64,32,128]{4,2,1,0,3:T(8,128)(2,1)} %convert_bitcast_fusion) | data formatting | bytes 4194304 | tf_op jit(solution)/shard_map/reshape | solution.py:24
  21.4 9.8 %reshape.35 = bf16[64,2,8192]{2,1,0:T(2,128)(2,1)} reshape(bf16[4096,2,2,64]{3,2,1,0:T(2,128)(2,1)} %bitcast.47) | data formatting | bytes 4194304
  31.3 9.2 %all-to-all-start = ((bf16[64,2,8192]{2,1,0:T(2,128)(2,1)}), bf16[64,2,8192]{2,1,0:T(2,128)(2,1)}, u32[]{:S(2)}, u32[]{:S(2)}) async-start(bf16[64,2,8192]{2,1,0:T(2,128)(2,1)} %reshape.35), calls=%async_computation | async-start | bytes 4194304 | tf_op jit(solution)/shard_map/all_to_all | solution.py:25
  40.7 1.4 broadcast_select_fusion
  42.2 0.9 copy.32
  43.2 24.6 %all-to-all-done = bf16[64,2,8192]{2,1,0:T(2,128)(2,1)} async-done(((bf16[64,2,8192]{2,1,0:T(2,128)(2,1)}), bf16[64,2,8192]{2,1,0:T(2,128)(2,1)}, u32[]{:S(2)}, u32[]{:S(2)}) %all-to-all-start) | async-done | bytes 2097184 | tf_op jit(solution)/shard_map/all_to_all | solution.py:25
  67.8 9.8 %reshape.36 = bf16[4096,2,2,64]{3,2,1,0:T(2,128)(2,1)} reshape(bf16[64,2,8192]{2,1,0:T(2,128)(2,1)} %all-to-all-done) | data formatting | bytes 4194304
  77.6 6.8 %copy.44 = bf16[2,2,64,64,64]{2,3,4,1,0:T(8,128)(2,1)} copy(bf16[2,2,64,64,64]{2,1,0,4,3:T(2,128)(2,1)} %bitcast.48) | data formatting | bytes 4194304 | tf_op jit(solution)/shard_map/all_to_all | solution.py:25
  84.4 6.2 %all_to_all.16 = bf16[2,2,32,128,64]{3,2,4,1,0:T(8,128)(2,1)} reshape(bf16[2,2,64,64,64]{3,2,4,1,0:T(8,128)(2,1)} %bitcast.49) | data formatting | bytes 4194304 | tf_op jit(solution)/shard_map/all_to_all | solution.py:25
  90.6 2.0 broadcast_multiply_fusion.1
  92.6 1.2 convolution_bitcast_fusion
  93.8 0.4 copy-done.3
  94.2 2.6 fusion.4
  96.9 0.7 all-gather.3.cloned.1.call-update
  97.6 1.6 broadcast_multiply_fusion
  99.2 53.3 %all-reduce.2.cloned.1.call-done = bf16[64,4096]{1,0:T(8,128)(2,1)} async-done(((bf16[64,4096]{1,0:T(8,128)(2,1)}), bf16[64,4096]{1,0:T(8,128)(2,1)}) %all-reduce.2.cloned.1.call-update) | async-done | bytes 524304 | tf_op jit(solution)/shard_map/psum | solution.py:32
  152.5 2.1 convert_element_type.25
  154.5 85.9 %all-gather.3.cloned.1.call-done = f32[256,4096]{1,0:T(8,128)} async-done(((f32[64,4096]{1,0:T(8,128)}), f32[256,4096]{1,0:T(8,128)}) %all-gather.3.cloned.1.call-update) | async-done | bytes 4194320 | tf_op jit(solution)/shard_map/all_gather | solution.py:18
  240.5 2.5 reduce_sum.28
  243.0 0.4 fusion.13
  243.4 1.2 copy-done.2
  244.8 5.9 %fusion.3 = f32[2,2,64,4096]{3,2,1,0:T(8,128)} fusion(bf16[2,2,64,4096]{3,2,1,0:T(8,128)(2,1)} %param.6, f32[32,2,2,8,8,128]{5,4,3,2,1,0:T(8,128)} %copy-done.1, f32[64,4096]{1,0:T(8,128)S(1)} %get-tuple-element.10, f32[64,4096]{1,0:T(8,128)S(1)} %copy-done.4, f32[2,64,4096]{2,1,0:T(8,128)S(1)} %copy-done.2, f32[64,4096]{1,0:T(8,128)S(1)} %get-tuple-element.9), kind=kLoop, calls=%fused_computation.7 | loop fusion | flops 6291456 | bytes 15728640 | tf_op jit(solution)/shard_map/add | solution.py:36
  (15 shorter events, 0.7 us)
Async XLA Ops:
  6.5 1.6 copy-start
  31.3 36.5 %all-to-all-start = ((bf16[64,2,8192]{2,1,0:T(2,128)(2,1)}), bf16[64,2,8192]{2,1,0:T(2,128)(2,1)}, u32[]{:S(2)}, u32[]{:S(2)}) async-start(bf16[64,2,8192]{2,1,0:T(2,128)(2,1)} %reshape.35), calls=%async_computation | async-start | bytes 4194304 | tf_op jit(solution)/shard_map/all_to_all | solution.py:25
  40.5 112.0 %all-reduce.2.cloned.1.call-start = ((), (), s32[]{:S(2)}) async-start(), calls=%async_computation.1 | async-start | bytes 1048576 | tf_op jit(solution)/shard_map/psum | solution.py:32
  90.6 2.0 copy-start.5
  92.6 1.6 copy-start.3
  92.6 1.6 copy-start.6
  94.2 2.6 copy-start.1
  96.8 143.6 %all-gather.3.cloned.1.call-start = ((), (), s32[]{:S(2)}) async-start(), calls=%async_computation.2 | async-start | bytes 5242880 | tf_op jit(solution)/shard_map/all_gather | solution.py:18
  243.0 1.6 copy-start.2
  243.0 1.8 copy-start.4
Sparse Core Ops, SparseCore 0:
  96.9 55.4 all-reduce.1
  154.3 86.1 all-gather.2

commit v2 on v0

--- a/solution.py
+++ b/solution.py
@@ -22,7 +22,10 @@
     blocks_x = seed_adjoint.reshape(con_local, 2, cols_local, nblocks, BLK)
     across = jnp.einsum("cpyki,kji->cpykj", blocks_x, inv_x, preferred_element_type=jnp.float32)
     across = across.astype(jnp.bfloat16).reshape(con_local, 2, cols_local, full_side)
-    arrived = lax.all_to_all(across, "grid", split_axis=3, concat_axis=2, tiled=True)
+    arrived = jnp.concatenate(
+        lax.all_to_all(jnp.stack(jnp.split(across, lax.axis_size("grid"), axis=3)), "grid", 0, 0),
+        axis=2,
+    )
     count = arrived.shape[0]
     masked = arrived * sea_turned[None, None]
     blocks_y = masked.reshape(count, 2, nblocks, BLK, rows_local)

time: 238 us -> 268 us (1.13)
  local copies, waits for them, and re-layouts: 45.7 us -> 77.5 us
    unnamed x15 -> x78, local copies, waits for them, and re-layouts: 22.7 us -> 63.4 us
    all_to_all x2 -> x0, local copies, waits for them, and re-layouts: 13 us -> none  [local(): lax.all_to_all(across, 'grid', split_axis=3, concat_axis=2, tiled=True)]
    reshape x0 -> x2, local copies, waits for them, and re-layouts: none -> 12.8 us  [local(): jnp.concatenate(lax.all_to_all(jnp.stack(jnp.split(across, lax.axis_size(...]
    reshape x1, local copies, waits for them, and re-layouts: 10 us -> 0.56 us  [local(): across.astype(jnp.bfloat16).reshape(con_local, 2, cols_local, full_side)]
where the time goes in v2:
time: 268 us; the launch traced here: 267 us
  waiting for transfers between devices  147 us (55%)
  local copies, waits for them, and re-layouts  77.5 us (29%)
  other arithmetic  16 us (6%)
  between operations  13.5 us (5%)
  starting transfers between devices  10.6 us (4%)
  matrix products  3.11 us (1%)
    psum x1, waiting for transfers between devices, local(): squares = lax.psum(local_squares, 'con')  68.7 us
    unnamed x78, local copies, waits for them, and re-layouts  63.4 us
    psum x1, waiting for transfers between devices, local(): lax.psum(local_inner.astype(jnp.bfloat16), 'con').astype(jnp.float32)  52.3 us
    all_to_all x1, waiting for transfers between devices, local(): lax.all_to_all(jnp.stack(jnp.split(across, lax.axis_size('grid'), axis=3)...  24.9 us
    reshape x2, local copies, waits for them, and re-layouts, local(): jnp.concatenate(lax.all_to_all(jnp.stack(jnp.split(across, lax.axis_size(...  12.8 us
    all_to_all x1, starting transfers between devices, local(): lax.all_to_all(jnp.stack(jnp.split(across, lax.axis_size('grid'), axis=3)...  10.5 us
    add x1, other arithmetic, local(): return first + second  5.88 us
  transfers between devices with their start and end apart: 3, of which 3 were waited for; matrix products, arithmetic and copies ran while one was open for 2% of the time, Pallas kernels for 0%

profile of v2, /device:TPU:1, one launch (start us, length us, event | category | flops | bytes accessed | tf_op | source)
XLA Modules:
  0.0 267.4 jit_solution(14310671882396429164)
XLA Ops:
  6.5 1.6 copy-done
  8.1 1.9 convert_bitcast_fusion
  14.0 0.7 constant_dynamic-update-slice_fusion.58
  18.1 0.7 constant_dynamic-update-slice_fusion.52
  19.5 0.7 constant_dynamic-update-slice_fusion.50
  23.6 0.7 constant_dynamic-update-slice_fusion.44
  54.4 7.9 %reshape.39 = bf16[64,2,8192]{2,1,0:T(2,128)(2,1)} reshape(bf16[64,2,2,64,64]{4,3,2,1,0:T(8,128)(2,1)} %constant_dynamic-update-slice_fusion) | data formatting | bytes 4194304
  62.3 10.5 %all-to-all-start = ((bf16[64,2,8192]{2,1,0:T(2,128)(2,1)}), bf16[64,2,8192]{2,1,0:T(2,128)(2,1)}, u32[]{:S(2)}, u32[]{:S(2)}) async-start(bf16[64,2,8192]{2,1,0:T(2,128)(2,1)} %reshape.39), calls=%async_computation | async-start | bytes 4194304 | tf_op jit(solution)/shard_map/all_to_all | solution.py:26
  72.9 1.4 broadcast_select_fusion
  74.4 0.9 copy.19
  75.3 24.9 %all-to-all-done = bf16[64,2,8192]{2,1,0:T(2,128)(2,1)} async-done(((bf16[64,2,8192]{2,1,0:T(2,128)(2,1)}), bf16[64,2,8192]{2,1,0:T(2,128)(2,1)}, u32[]{:S(2)}, u32[]{:S(2)}) %all-to-all-start) | async-done | bytes 2097184 | tf_op jit(solution)/shard_map/all_to_all | solution.py:26
  100.3 7.9 %reshape.40 = bf16[64,2,2,64,64]{4,3,2,1,0:T(8,128)(2,1)} reshape(bf16[64,2,8192]{2,1,0:T(2,128)(2,1)} %all-to-all-done) | data formatting | bytes 4194304
  108.2 6.6 %copy.11 = bf16[2,2,64,64,64]{3,2,4,1,0:T(8,128)(2,1)} copy(bf16[2,2,64,64,64]{4,3,1,0,2:T(8,128)(2,1)} %bitcast.364) | data formatting | bytes 4194304 | tf_op jit(solution)/shard_map/reshape | solution.py:25
  114.8 6.2 %reshape.34 = bf16[2,2,32,128,64]{3,2,4,1,0:T(8,128)(2,1)} reshape(bf16[2,2,64,64,64]{3,2,4,1,0:T(8,128)(2,1)} %copy.11) | data formatting | bytes 4194304 | tf_op jit(solution)/shard_map/reshape | solution.py:25
  121.0 2.0 broadcast_multiply_fusion.1
  123.0 1.2 convolution_bitcast_fusion
  124.2 1.9 copy-done.1
  126.1 2.1 fusion.4
  129.0 1.6 broadcast_multiply_fusion
  130.6 52.3 %all-reduce.5.cloned.1.call-done = bf16[64,4096]{1,0:T(8,128)(2,1)} async-done(((bf16[64,4096]{1,0:T(8,128)(2,1)}), bf16[64,4096]{1,0:T(8,128)(2,1)}) %all-reduce.5.cloned.1.call-update) | async-done | bytes 524304 | tf_op jit(solution)/shard_map/psum | solution.py:35
  182.9 1.1 convert_element_type.25
  184.0 68.7 %all-reduce.3.cloned.1.call-done = f32[64,4096]{1,0:T(8,128)} async-done(((f32[64,4096]{1,0:T(8,128)}), f32[64,4096]{1,0:T(8,128)}) %all-reduce.3.cloned.1.call-update) | async-done | bytes 1048592 | tf_op jit(solution)/shard_map/psum | solution.py:18
  252.8 1.8 fusion.13
  254.7 5.9 %fusion.3 = f32[2,2,64,4096]{3,2,1,0:T(8,128)} fusion(bf16[2,2,64,4096]{3,2,1,0:T(8,128)(2,1)} %param.6, f32[32,2,2,8,8,128]{5,4,3,2,1,0:T(8,128)} %copy-done.1, f32[64,4096]{1,0:T(8,128)S(1)} %get-tuple-element.10, f32[64,4096]{1,0:T(8,128)S(1)} %convert_element_type.25, f32[2,64,4096]{2,1,0:T(8,128)S(1)} %copy-done.2, f32[64,4096]{1,0:T(8,128)S(1)} %get-tuple-element.9), kind=kLoop, calls=%fused_computation.7 | loop fusion | flops 6291456 | bytes 15728640 | tf_op jit(solution)/shard_map/add | solution.py:39
  (76 shorter events, 42.5 us)
Async XLA Ops:
  6.5 1.6 copy-start
  62.3 38.0 %all-to-all-start = ((bf16[64,2,8192]{2,1,0:T(2,128)(2,1)}), bf16[64,2,8192]{2,1,0:T(2,128)(2,1)}, u32[]{:S(2)}, u32[]{:S(2)}) async-start(bf16[64,2,8192]{2,1,0:T(2,128)(2,1)} %reshape.39), calls=%async_computation | async-start | bytes 4194304 | tf_op jit(solution)/shard_map/all_to_all | solution.py:26
  72.8 110.1 %all-reduce.5.cloned.1.call-start = ((), (), s32[]{:S(2)}) async-start(), calls=%async_computation.2 | async-start | bytes 1048576 | tf_op jit(solution)/shard_map/psum | solution.py:35
  121.0 2.0 copy-start.4
  123.0 3.1 %copy-start.3 = (bf16[2,2,64,4096]{3,2,1,0:T(8,128)(2,1)S(1)}, bf16[2,2,64,4096]{3,2,1,0:T(8,128)(2,1)}, u32[]{:S(2)}) copy-start(bf16[2,2,64,4096]{3,2,1,0:T(8,128)(2,1)} %param.6) | copy-start | bytes 6291460
  123.0 3.1 %copy-start.5 = (f32[2]{0:T(128)S(1)}, f32[2]{0:T(128)}, u32[]{:S(2)}) copy-start(f32[2]{0:T(128)} %param.11) | copy-start | bytes 28
  124.2 1.9 copy-start.1
  128.2 124.5 %all-reduce.3.cloned.1.call-start = ((), (), s32[]{:S(2)}) async-start(), calls=%async_computation.1 | async-start | bytes 2097152 | tf_op jit(solution)/shard_map/psum | solution.py:18
  252.8 1.9 copy-start.2
Sparse Core Ops, SparseCore 0:
  128.4 54.5 all-reduce.4
  185.6 67.1 all-reduce.2
